TPU v7x, 32 devices: a whole 2x2x4 slice. The times are simulated.
32 devices in a mesh: req: 8 (over y, x, core), tp: 4 (over z).
Axes of the slice: x: 2, y: 2, z: 4, core: 2. Of those that a mesh axis runs over, the one named last changes fastest.
Arguments:
- residual: bfloat16 [2048, 2048], P('req', 'tp'), may hold values from -0.29882812 to 0.29882812
- queries: bfloat16 [2048, 1280], P('req', 'tp'), may hold values from -6 to 6
- suffix_kv: bfloat16 [2048, 4, 256], P('req', 'tp'), may hold values from -4 to 4
- prefix_cache: bfloat16 [8192, 4, 256], P('req', 'tp'), may hold values from -6 to 6
- out_weight: bfloat16 [1280, 2048], P('tp'), may hold values from -0.15625 to 0.15625
- norm_gain: bfloat16 [2048], replicated, may hold values from 0.5 to 1.5
- next_query_weight: bfloat16 [2048, 1280], P(None, 'tp'), may hold values from -0.125 to 0.125
- lengths: int32 [8, 4], P('req'), may hold values from 1 to 128, 256 in all within a row
- tenant: int32 [8, 4], P('req'), may hold values from 0 to 3
- owners: int32 [4], replicated, may hold values from 0 to 7, as said below
Outputs:
- new_residual: bfloat16 [2048, 2048], P('req', 'tp')
- next_queries: bfloat16 [2048, 1280], P('req', 'tp')
Inputs may be any that keep to these rules, and one draw needn't show every extreme that they name: `lengths`: each device's 4 requests fill its 256 rows in order. `owners`: distinct.
All inputs are finite; a program needn't handle non-finite values.
Results may differ from a plain program's by a relative error of at most 0.0065.
Values may be sent and summed in bfloat16 or wider, within the bound.
No kernel may reach another device: no remote copies, remote signals or barrier semaphores. Data moves between devices by JAX's collectives and lax.ppermute only.
A program may use at most 64 MiB of HBM per device.

v0:
```python
import jax
import jax.numpy as jnp
from jax import lax
from jax.sharding import PartitionSpec as P

QH = 20
KVH = 5
HD = 64
TENANTS = 4
GATHER_SLOTS_MAX = 16


def from_root(block, axis, source):
    block = jnp.where(lax.axis_index(axis) == source, block, jnp.zeros_like(block))
    return lax.psum(block, axis)


def pick_heads(pair_rows, select):
    split_pair = pair_rows.reshape(pair_rows.shape[0], 2, 2, HD)
    key_heads = jnp.einsum(
        "njd,hj->nhd", split_pair[:, :, 0], select, preferred_element_type=jnp.float32
    ).astype(jnp.bfloat16)
    value_heads = jnp.einsum(
        "njd,hj->nhd", split_pair[:, :, 1], select, preferred_element_type=jnp.float32
    ).astype(jnp.bfloat16)
    return (key_heads, value_heads)


def every_slot_of(part, n_req):
    return lax.all_gather(part, "req", axis=0, tiled=True)


def slots_of_tenants(part, every_slot, owners, n_req):
    slot_rows = part.shape[0]
    if n_req <= GATHER_SLOTS_MAX:
        return [
            lax.dynamic_slice_in_dim(every_slot, owners[tenant_id] * slot_rows, slot_rows, 0)
            for tenant_id in range(TENANTS)
        ]
    return [from_root(part, "req", owners[tenant_id]) for tenant_id in range(TENANTS)]


def pick_part(part_rows, select):
    return jnp.einsum("njd,hj->nhd", part_rows, select, preferred_element_type=jnp.float32).astype(
        jnp.bfloat16
    )


def shifted(block, shift, n_tp):
    pairs = [(source, (source + shift) % n_tp) for source in range(n_tp)]
    return lax.ppermute(block, "tp", pairs)


def local(
    residual,
    queries,
    suffix_kv,
    prefix_cache,
    out_weight,
    norm_gain,
    next_query_weight,
    lengths,
    tenant,
    owners,
    n_req,
    n_tp,
):
    row_count = queries.shape[0]
    head_count = queries.shape[1] // HD
    width = residual.shape[1]
    tp_index = lax.axis_index("tp")
    weight_pieces = []
    for shift in range(n_tp):
        target = (tp_index + shift) % n_tp
        piece = lax.dynamic_slice_in_dim(out_weight, target * width, width, 1)
        weight_pieces.append(piece if shift == 0 else shifted(piece, shift, n_tp))
    head_ids = tp_index * head_count + jnp.arange(head_count, dtype=jnp.int32)
    pair_ids = head_ids // (QH // KVH) - tp_index
    select = (pair_ids[:, None] == jnp.arange(2, dtype=jnp.int32)[None, :]).astype(jnp.bfloat16)
    req_lengths = lengths[0]
    req_tenant = tenant[0]
    req_ends = jnp.cumsum(req_lengths)
    req_starts = req_ends - req_lengths
    position = jnp.arange(row_count, dtype=jnp.int32)
    request_ids = jnp.sum((position[:, None] >= req_ends[None, :]).astype(jnp.int32), axis=1)
    member = request_ids[:, None] == jnp.arange(req_lengths.shape[0], dtype=jnp.int32)[None, :]
    row_start = jnp.sum(jnp.where(member, req_starts[None, :], 0), axis=1)
    row_tenant = jnp.sum(jnp.where(member, req_tenant[None, :], 0), axis=1)
    score_scale = HD ** (-0.5)
    query_heads = queries.reshape(row_count, head_count, HD)
    suffix_keys, suffix_values = pick_heads(suffix_kv.reshape(row_count, -1), select)
    suffix_scores = (
        jnp.einsum("rhd,khd->hrk", query_heads, suffix_keys, preferred_element_type=jnp.float32)
        * score_scale
    )
    suffix_mask = (
        (position[None, :] >= row_start[:, None]) & (position[None, :] <= position[:, None])
    )[None]
    own_slot = prefix_cache.reshape(prefix_cache.shape[0], 2, 2, HD)
    own_keys = own_slot[:, :, 0]
    own_values = own_slot[:, :, 1]
    if n_req <= GATHER_SLOTS_MAX:
        every_key = every_slot_of(own_keys, n_req)
        own_values, every_key = lax.optimization_barrier((own_values, every_key))
        every_value = every_slot_of(own_values, n_req)
    else:
        every_key = every_value = None
    key_blocks = slots_of_tenants(own_keys, every_key, owners, n_req)
    value_blocks = slots_of_tenants(own_values, every_value, owners, n_req)
    picked = [
        (pick_part(key_rows, select), pick_part(value_rows, select))
        for key_rows, value_rows in zip(key_blocks, value_blocks)
    ]
    row_top = jnp.max(jnp.where(suffix_mask, suffix_scores, -jnp.inf), axis=2)
    for tenant_id in range(TENANTS):
        tenant_mask = (row_tenant == tenant_id)[None, :, None]
        prefix_scores = (
            jnp.einsum(
                "rhd,phd->hrp",
                query_heads,
                picked[tenant_id][0],
                preferred_element_type=jnp.float32,
            )
            * score_scale
        )
        row_top = jnp.maximum(
            row_top, jnp.max(jnp.where(tenant_mask, prefix_scores, -jnp.inf), axis=2)
        )
    suffix_weights = jnp.where(suffix_mask, jnp.exp(suffix_scores - row_top[:, :, None]), 0.0)
    denominator = jnp.sum(suffix_weights, axis=2)
    accumulated = jnp.einsum(
        "hrk,khd->rhd",
        suffix_weights.astype(jnp.bfloat16),
        suffix_values,
        preferred_element_type=jnp.float32,
    )
    for tenant_id in range(TENANTS):
        tenant_mask = (row_tenant == tenant_id)[None, :, None]
        prefix_scores = (
            jnp.einsum(
                "rhd,phd->hrp",
                query_heads,
                picked[tenant_id][0],
                preferred_element_type=jnp.float32,
            )
            * score_scale
        )
        prefix_weights = jnp.where(tenant_mask, jnp.exp(prefix_scores - row_top[:, :, None]), 0.0)
        denominator = denominator + jnp.sum(prefix_weights, axis=2)
        accumulated = accumulated + jnp.einsum(
            "hrp,phd->rhd",
            prefix_weights.astype(jnp.bfloat16),
            picked[tenant_id][1],
            preferred_element_type=jnp.float32,
        )
    attended = (
        (accumulated / jnp.transpose(denominator)[:, :, None])
        .astype(jnp.bfloat16)
        .reshape(row_count, -1)
    )
    projected = jnp.dot(attended, weight_pieces[0], preferred_element_type=jnp.float32)
    for shift in range(1, n_tp):
        head_block = shifted(attended, shift, n_tp)
        projected = projected + jnp.dot(
            head_block, weight_pieces[shift], preferred_element_type=jnp.float32
        )
    new_residual = (residual.astype(jnp.float32) + projected).astype(jnp.bfloat16)
    full_new = lax.all_gather(new_residual, "tp", axis=1, tiled=True)
    widened = full_new.astype(jnp.float32)
    mean_square = jnp.mean(widened * widened, axis=1, keepdims=True)
    normed = (widened * lax.rsqrt(mean_square + 1e-05) * norm_gain.astype(jnp.float32)).astype(
        jnp.bfloat16
    )
    next_sums = jnp.dot(normed, next_query_weight, preferred_element_type=jnp.float32)
    return (new_residual, next_sums.astype(jnp.bfloat16))


def solution(mesh):
    n_req = mesh.shape["req"]
    n_tp = mesh.shape["tp"]

    def body(*args):
        return local(*args, n_req=n_req, n_tp=n_tp)

    return jax.shard_map(
        body,
        mesh=mesh,
        in_specs=(
            P("req", "tp"),
            P("req", "tp"),
            P("req", "tp", None),
            P("req", "tp", None),
            P("tp", None),
            P(),
            P(None, "tp"),
            P("req", None),
            P("req", None),
            P(),
        ),
        out_specs=(P("req", "tp"), P("req", "tp")),
        check_vma=False,
    )
```

profile of v0, /device:TPU:0, one launch (start us, length us, event | category | flops | bytes accessed | tf_op | source)
XLA Modules:
  0.0 150.9 jit_solution(15637092772348222072)
XLA Ops:
  7.2 0.0 copy-start
  7.2 0.0 all-gather.9.cloned.1.call-start
  7.2 1.4 copy.28
  8.6 0.7 fusion.107
  9.4 0.0 all-gather.9.cloned.1.call-update
  9.4 0.0 all-gather.5.cloned.1.call-start
  9.5 2.2 %constant_dynamic-slice_fusion.1 = (bf16[320,512]{1,0:T(8,128)(2,1)}, bf16[320,512]{1,0:T(8,128)(2,1)}, bf16[320,512]{1,0:T(8,128)(2,1)}) fusion(bf16[320,2048]{1,0:T(8,128)(2,1)} %param.14, s32[]{:T(128)S(6)} %select_n.137, s32[]{:T(128)S(6)} %select_n.135, s32[]{:T(128)S(6)} %select_n.139), kind=kLoop, calls=%fused_computation.113 | loop fusion | bytes 1966092 | tf_op jit(solution)/shard_map/dynamic_slice | solution.py:75
  11.7 3.0 %collective-permute-start.1 = (bf16[320,512]{1,0:T(8,128)(2,1)}, bf16[320,512]{1,0:T(8,128)(2,1)}, u32[]{:S(2)}, u32[]{:S(2)}) collective-permute-start(bf16[320,512]{1,0:T(8,128)(2,1)} %get-tuple-element.13), channel_id=1, source_target_pairs={{0,1},{1,2},{2,3},{3,0},{4,5},{5,6},{6,7},{7,4},{8,9},{9,10},{10,1... | collective-permute-start | bytes 983048 | tf_op jit(solution)/shard_map/ppermute | solution.py:51
  14.7 2.0 %collective-permute-start.5 = (bf16[320,512]{1,0:T(8,128)(2,1)}, bf16[320,512]{1,0:T(8,128)(2,1)}, u32[]{:S(2)}, u32[]{:S(2)}) collective-permute-start(bf16[320,512]{1,0:T(8,128)(2,1)} %get-tuple-element.14), channel_id=1, source_target_pairs={{0,3},{1,0},{2,1},{3,2},{4,7},{5,4},{6,5},{7,6},{8,11},{9,8},{10,9... | collective-permute-start | bytes 983048 | tf_op jit(solution)/shard_map/ppermute | solution.py:51
  16.7 1.0 collective-permute-start.3
  17.7 1.5 fusion.108
  21.8 0.8 reduce-window.4
  22.6 1.0 copy.24
  23.7 0.1 convert_reduce_fusion
  23.8 0.7 fusion.86
  24.4 0.7 select_reduce_fusion.6
  25.3 0.3 fusion.29
  25.5 1.0 fusion.28
  26.5 0.4 select_reduce_fusion.4
  26.9 14.2 %all-gather.9.cloned.1.call-done = bf16[8192,2,1,64]{0,3,2,1:T(8,128)(2,1)} async-done(((bf16[1024,2,1,64]{0,3,2,1:T(8,128)(2,1)}), bf16[8192,2,1,64]{0,3,2,1:T(8,128)(2,1)}) %all-gather.9.cloned.1.call-update) | async-done | bytes 2097168 | tf_op jit(solution)/shard_map/all_gather | solution.py:30
  41.1 3.8 %copy.29 = bf16[8192,2,64]{0,1,2:T(2,128)(2,1)S(1)} copy(bf16[8192,2,64]{0,2,1:T(8,128)(2,1)} %bitcast.115) | data formatting | bytes 4194304 | tf_op jit(solution)/shard_map/optimization_barrier | solution.py:104
  44.9 1.6 %fusion.14 = bf16[1024,5,64]{0,1,2:T(8,128)(2,1)} fusion(bf16[8192,2,64]{0,1,2:T(2,128)(2,1)S(1)} %copy.29, s32[]{:T(128)S(6)} %select_n.119, s32[5]{0:T(128)S(1)} %fusion.97), kind=kOutput, calls=%fused_computation.41 | convolution fusion | flops 1638410 | bytes 918020 | tf_op jit(solution)/shard_map/njd,hj->nhd/dot_general | solution.py:44
  46.5 1.5 %fusion.13 = bf16[1024,5,64]{0,1,2:T(8,128)(2,1)} fusion(bf16[8192,2,64]{0,1,2:T(2,128)(2,1)S(1)} %copy.29, s32[]{:T(128)S(6)} %select_n.117, s32[5]{0:T(128)S(1)} %fusion.97), kind=kOutput, calls=%fused_computation.40 | convolution fusion | flops 1638410 | bytes 918020 | tf_op jit(solution)/shard_map/njd,hj->nhd/dot_general | solution.py:44
  48.1 1.5 %fusion.12 = bf16[1024,5,64]{0,1,2:T(8,128)(2,1)} fusion(bf16[8192,2,64]{0,1,2:T(2,128)(2,1)S(1)} %copy.29, s32[]{:T(128)S(6)} %select_n.115, s32[5]{0:T(128)S(1)} %fusion.97), kind=kOutput, calls=%fused_computation.39 | convolution fusion | flops 1638410 | bytes 918020 | tf_op jit(solution)/shard_map/njd,hj->nhd/dot_general | solution.py:44
  49.6 1.0 copy.39
  50.6 0.0 all-gather.5.cloned.1.call-update
  50.6 0.2 all-gather.7.cloned.1.call-start
  50.8 1.6 %fusion.15 = bf16[1024,5,64]{0,1,2:T(8,128)(2,1)S(1)} fusion(bf16[8192,2,64]{0,1,2:T(2,128)(2,1)} %copy-done.5, s32[]{:T(128)S(6)} %select_n.121, s32[5]{0:T(128)S(1)} %fusion.97), kind=kOutput, calls=%fused_computation.42 | convolution fusion | flops 1638410 | bytes 917528 | tf_op jit(solution)/shard_map/njd,hj->nhd/dot_general | solution.py:44
  52.4 2.7 %select_reduce_fusion.1 = (f32[5,256]{1,0:T(8,128)S(1)}, f32[5,1024,256]{2,1,0:T(8,128)S(1)}) fusion(pred[256]{0:T(512)(128)(4,1)S(1)} %get-tuple-element.21, bf16[256,5,64]{0,2,1:T(8,128)(2,1)S(1)} %bitcast.111, bf16[1024,5,64]{0,1,2:T(8,128)(2,1)} %fusion.14), kind=kOutput, calls=%fused_computation.13 | convolution fusion | flops 171703040 | bytes 6067456 | tf_op jit(solution)/shard_map/rhd,phd->hrp/dot_general | solution.py:118
  55.1 1.3 select_reduce_fusion.2
  56.5 1.3 select_reduce_fusion.3
  57.9 1.3 select_reduce_fusion
  59.3 0.2 fusion.31
  59.5 4.4 %bitcast_reduce_fusion.3 = (f32[5,256]{1,0:T(8,128)S(1)}, f32[5,256]{1,0:T(8,128)S(1)}, f32[5,256]{1,0:T(8,128)S(1)}, f32[5,256]{1,0:T(8,128)S(1)}) fusion(f32[5,1024,256]{2,1,0:T(8,128)S(1)} %get-tuple-element.36, f32[5,256]{1,0:T(8,128)S(1)} %maximum_maximum_fusion, pred[256]{0:T(512)(128)(4,1)S(1)} %get-tuple-element.19, ...), kind=kLoop, calls=%fused_computation.6 | loop fusion | flops 20966400 | bytes 20998144 | tf_op jit(solution)/shard_map/reduce_sum | solution.py:149
  64.0 15.0 %all-gather.5.cloned.1.call-done = bf16[8192,2,64]{0,1,2:T(2,128)(2,1)} async-done(((bf16[1024,2,64]{0,1,2:T(2,128)(2,1)}), bf16[8192,2,64]{0,1,2:T(2,128)(2,1)}) %all-gather.5.cloned.1.call-update) | async-done | bytes 2097168 | tf_op jit(solution)/shard_map/all_gather | solution.py:30
  78.9 1.6 %fusion.16 = bf16[1024,5,64]{0,1,2:T(8,128)(2,1)S(1)} fusion(bf16[8192,2,64]{0,1,2:T(2,128)(2,1)} %all-gather.5.cloned.1.call-done, s32[]{:T(128)S(6)} %select_n.115, s32[5]{0:T(128)S(1)} %fusion.97), kind=kOutput, calls=%fused_computation.43 | convolution fusion | flops 1638410 | bytes 917528 | tf_op jit(solution)/shard_map/njd,hj->nhd/dot_general | solution.py:44
  80.6 0.0 slice-start.5
  80.6 4.1 %fusion = f32[5,64,256]{2,1,0:T(8,128)S(1)} fusion(f32[5,1024,256]{2,1,0:T(8,128)} %copy-done.4, f32[5,256]{1,0:T(8,128)S(1)} %maximum_maximum_fusion, pred[256]{0:T(512)(128)(4,1)S(1)} %get-tuple-element.19, bf16[1024,5,64]{0,1,2:T(8,128)(2,1)S(1)} %fusion.16), kind=kOutput, calls=%fused_computation.18 | convolution fusion | flops 173015040 | bytes 6231296 | tf_op jit(solution)/shard_map/hrp,phd->rhd/dot_general | solution.py:150
  84.7 1.6 %fusion.17 = bf16[1024,5,64]{0,1,2:T(8,128)(2,1)S(1)} fusion(bf16[8192,2,64]{0,1,2:T(2,128)(2,1)} %all-gather.5.cloned.1.call-done, s32[]{:T(128)S(6)} %select_n.117, s32[5]{0:T(128)S(1)} %fusion.97), kind=kOutput, calls=%fused_computation.44 | convolution fusion | flops 1638410 | bytes 917528 | tf_op jit(solution)/shard_map/njd,hj->nhd/dot_general | solution.py:44
  86.3 0.0 slice-start.1
  86.3 1.4 fusion.1
  87.8 1.6 %fusion.18 = bf16[1024,5,64]{0,1,2:T(8,128)(2,1)S(1)} fusion(bf16[8192,2,64]{0,1,2:T(2,128)(2,1)} %all-gather.5.cloned.1.call-done, s32[]{:T(128)S(6)} %select_n.119, s32[5]{0:T(128)S(1)} %fusion.97), kind=kOutput, calls=%fused_computation.45 | convolution fusion | flops 1638410 | bytes 917528 | tf_op jit(solution)/shard_map/njd,hj->nhd/dot_general | solution.py:44
  89.4 0.0 slice-start.3
  89.5 1.4 fusion.2
  90.9 1.5 %fusion.19 = bf16[1024,5,64]{0,1,2:T(8,128)(2,1)S(1)} fusion(bf16[8192,2,64]{0,1,2:T(2,128)(2,1)} %all-gather.5.cloned.1.call-done, s32[]{:T(128)S(6)} %select_n.121, s32[5]{0:T(128)S(1)} %fusion.97), kind=kOutput, calls=%fused_computation.46 | convolution fusion | flops 1638410 | bytes 917528 | tf_op jit(solution)/shard_map/njd,hj->nhd/dot_general | solution.py:44
  92.5 1.4 fusion.3
  93.9 0.0 copy-start.11
  93.9 0.3 fusion.30
  94.3 1.5 %collective-permute-start = (bf16[256,320]{0,1:T(8,128)(2,1)S(1)}, bf16[256,320]{0,1:T(8,128)(2,1)S(1)}, u32[]{:S(2)}, u32[]{:S(2)}) collective-permute-start(bf16[256,320]{0,1:T(8,128)(2,1)S(1)} %bitcast.118), channel_id=1, source_target_pairs={{0,1},{1,2},{2,3},{3,0},{4,5},{5,6},{6,7},{7,4},{8,9},{9,10},{10,1... | collective-permute-start | bytes 491528 | tf_op jit(solution)/shard_map/ppermute | solution.py:51
  95.8 2.3 %collective-permute-start.4 = (bf16[256,320]{0,1:T(8,128)(2,1)S(1)}, bf16[256,320]{0,1:T(8,128)(2,1)S(1)}, u32[]{:S(2)}, u32[]{:S(2)}) collective-permute-start(bf16[256,320]{0,1:T(8,128)(2,1)S(1)} %bitcast.119), channel_id=1, source_target_pairs={{0,3},{1,0},{2,1},{3,2},{4,7},{5,4},{6,5},{7,6},{8,11},{9,8},{10,9... | collective-permute-start | bytes 491528 | tf_op jit(solution)/shard_map/ppermute | solution.py:51
  98.1 1.3 fusion.52
  99.5 0.7 collective-permute-start.2
  100.1 3.1 %collective-permute-done = bf16[256,320]{0,1:T(8,128)(2,1)S(1)} collective-permute-done((bf16[256,320]{0,1:T(8,128)(2,1)S(1)}, bf16[256,320]{0,1:T(8,128)(2,1)S(1)}, u32[]{:S(2)}, u32[]{:S(2)}) %collective-permute-start) | collective-permute-done | bytes 163872 | tf_op jit(solution)/shard_map/ppermute | solution.py:51
  103.2 1.3 convolution_add_fusion.1
  104.5 0.0 collective-permute-done.5
  104.5 0.9 collective-permute-done.4
  105.4 1.3 fusion.109
  106.7 0.0 collective-permute-done.3
  106.7 6.3 %collective-permute-done.2 = bf16[256,320]{0,1:T(8,128)(2,1)S(1)} collective-permute-done((bf16[256,320]{0,1:T(8,128)(2,1)S(1)}, bf16[256,320]{0,1:T(8,128)(2,1)S(1)}, u32[]{:S(2)}, u32[]{:S(2)}) %collective-permute-start.2) | collective-permute-done | bytes 163872 | tf_op jit(solution)/shard_map/ppermute | solution.py:51
  113.0 1.0 fusion.22
  114.1 0.0 all-gather.7.cloned.1.call-update
  114.1 26.2 %all-gather.7.cloned.1.call-done = bf16[256,2048]{1,0:T(8,128)(2,1)} async-done(((bf16[256,512]{1,0:T(8,128)(2,1)}), bf16[256,2048]{1,0:T(8,128)(2,1)}) %all-gather.7.cloned.1.call-update) | async-done | bytes 1048592 | tf_op jit(solution)/shard_map/all_gather | solution.py:168
  140.4 1.5 fusion.8
  141.9 2.5 %convolution_convert_fusion.10 = bf16[256,320]{0,1:T(8,128)(2,1)} fusion(bf16[2048,320]{0,1:T(8,128)(2,1)S(1)} %copy-done, bf16[256,2048]{1,0:T(8,128)(2,1)} %all-gather.7.cloned.1.call-done, f32[2048]{0:T(1024)S(1)} %convert_element_type.130, f32[256]{0:T(256)S(1)} %add_rsqrt_fusion), kind=kOutput, calls=%fused_computation.65 | convolution fusion | flops 337723392 | bytes 2532352 | tf_op jit(solution)/shard_map/dot_general | solution.py:174
  (43 shorter events, 0.2 us)
Async XLA Ops:
  7.2 134.7 %copy-start = (bf16[2048,320]{0,1:T(8,128)(2,1)S(1)}, bf16[2048,320]{0,1:T(8,128)(2,1)}, u32[]{:S(2)}) copy-start(bf16[2048,320]{0,1:T(8,128)(2,1)} %param.16) | copy-start | bytes 3932164
  7.2 19.3 %copy-start.6 = (bf16[256,320]{0,1:T(8,128)(2,1)S(1)}, bf16[256,320]{0,1:T(8,128)(2,1)}, u32[]{:S(2)}) copy-start(bf16[256,320]{0,1:T(8,128)(2,1)} %param.11) | copy-start | bytes 491524
  7.2 33.9 %all-gather.9.cloned.1.call-start = ((), (), s32[]{:S(2)}) async-start(), calls=%async_computation.2 | async-start | bytes 2359296 | tf_op jit(solution)/shard_map/all_gather | solution.py:30
  9.4 69.6 %all-gather.5.cloned.1.call-start = ((), (), s32[]{:S(2)}) async-start(), calls=%async_computation | async-start | bytes 2359296 | tf_op jit(solution)/shard_map/all_gather | solution.py:30
  11.7 87.8 %collective-permute-start.1 = (bf16[320,512]{1,0:T(8,128)(2,1)}, bf16[320,512]{1,0:T(8,128)(2,1)}, u32[]{:S(2)}, u32[]{:S(2)}) collective-permute-start(bf16[320,512]{1,0:T(8,128)(2,1)} %get-tuple-element.13), channel_id=1, source_target_pairs={{0,1},{1,2},{2,3},{3,0},{4,5},{5,6},{6,7},{7,4},{8,9},{9,10},{10,1... | collective-permute-start | bytes 983048 | tf_op jit(solution)/shard_map/ppermute | solution.py:51
  14.7 89.8 %collective-permute-start.5 = (bf16[320,512]{1,0:T(8,128)(2,1)}, bf16[320,512]{1,0:T(8,128)(2,1)}, u32[]{:S(2)}, u32[]{:S(2)}) collective-permute-start(bf16[320,512]{1,0:T(8,128)(2,1)} %get-tuple-element.14), channel_id=1, source_target_pairs={{0,3},{1,0},{2,1},{3,2},{4,7},{5,4},{6,5},{7,6},{8,11},{9,8},{10,9... | collective-permute-start | bytes 983048 | tf_op jit(solution)/shard_map/ppermute | solution.py:51
  16.7 90.0 %collective-permute-start.3 = (bf16[320,512]{1,0:T(8,128)(2,1)}, bf16[320,512]{1,0:T(8,128)(2,1)S(1)}, u32[]{:S(2)}, u32[]{:S(2)}) collective-permute-start(bf16[320,512]{1,0:T(8,128)(2,1)} %get-tuple-element.12), channel_id=1, source_target_pairs={{0,2},{1,3},{2,0},{3,1},{4,6},{5,7},{6,4},{7,5},{8,10},{9,11},{10,... | collective-permute-start | bytes 983048 | tf_op jit(solution)/shard_map/ppermute | solution.py:51
  44.9 3.2 %copy-start.5 = (bf16[8192,2,64]{0,1,2:T(2,128)(2,1)}, bf16[8192,2,64]{0,1,2:T(2,128)(2,1)S(1)}, u32[]{:S(2)}) copy-start(bf16[8192,2,64]{0,1,2:T(2,128)(2,1)S(1)} %copy.29) | copy-start | bytes 6291460
  50.6 89.8 %all-gather.7.cloned.1.call-start = ((), (), s32[]{:S(2)}) async-start(), calls=%async_computation.1 | async-start | bytes 1310720 | tf_op jit(solution)/shard_map/all_gather | solution.py:168
  50.8 4.3 %copy-start.8 = (bf16[1024,5,64]{0,1,2:T(8,128)(2,1)S(1)}, bf16[1024,5,64]{0,1,2:T(8,128)(2,1)}, u32[]{:S(2)}) copy-start(bf16[1024,5,64]{0,1,2:T(8,128)(2,1)} %fusion.13) | copy-start | bytes 1966084
  52.4 4.1 %copy-start.7 = (bf16[1024,5,64]{0,1,2:T(8,128)(2,1)S(1)}, bf16[1024,5,64]{0,1,2:T(8,128)(2,1)}, u32[]{:S(2)}) copy-start(bf16[1024,5,64]{0,1,2:T(8,128)(2,1)} %fusion.12) | copy-start | bytes 1966084
  55.1 4.4 %copy-start.1 = (f32[5,1024,256]{2,1,0:T(8,128)}, f32[5,1024,256]{2,1,0:T(8,128)S(1)}, u32[]{:S(2)}) copy-start(f32[5,1024,256]{2,1,0:T(8,128)S(1)} %get-tuple-element.30) | copy-start | bytes 15728644
  56.5 3.0 %copy-start.3 = (f32[5,1024,256]{2,1,0:T(8,128)}, f32[5,1024,256]{2,1,0:T(8,128)S(1)}, u32[]{:S(2)}) copy-start(f32[5,1024,256]{2,1,0:T(8,128)S(1)} %get-tuple-element.32) | copy-start | bytes 15728644
  57.9 6.1 %copy-start.4 = (f32[5,1024,256]{2,1,0:T(8,128)}, f32[5,1024,256]{2,1,0:T(8,128)S(1)}, u32[]{:S(2)}) copy-start(f32[5,1024,256]{2,1,0:T(8,128)S(1)} %get-tuple-element.36) | copy-start | bytes 15728644
  59.2 4.7 %copy-start.2 = (f32[5,1024,256]{2,1,0:T(8,128)}, f32[5,1024,256]{2,1,0:T(8,128)S(1)}, u32[]{:S(2)}) copy-start(f32[5,1024,256]{2,1,0:T(8,128)S(1)} %get-tuple-element.28) | copy-start | bytes 15728644
  78.9 7.4 %slice-start.4 = ((s8[5242880]{0:T(1024)(128)(4,1)}), s8[4194304]{0:T(1024)(128)(4,1)S(1)}, s32[]{:S(2)}) async-start(s8[5242880]{0:T(1024)(128)(4,1)} %bitcast.108), calls=%async_computation.7 | async-start | bytes 8388608
  80.6 5.7 %slice-start.5 = ((s8[5242880]{0:T(1024)(128)(4,1)}), s8[1048576]{0:T(1024)(128)(4,1)S(1)}, s32[]{:S(2)}) async-start(s8[5242880]{0:T(1024)(128)(4,1)} %bitcast.108), calls=%async_computation.8 | async-start | bytes 2097152
  84.7 4.8 %slice-start = ((s8[5242880]{0:T(1024)(128)(4,1)}), s8[4194304]{0:T(1024)(128)(4,1)S(1)}, s32[]{:S(2)}) async-start(s8[5242880]{0:T(1024)(128)(4,1)} %bitcast.104), calls=%async_computation.3 | async-start | bytes 8388608
  86.3 3.1 %slice-start.1 = ((s8[5242880]{0:T(1024)(128)(4,1)}), s8[1048576]{0:T(1024)(128)(4,1)S(1)}, s32[]{:S(2)}) async-start(s8[5242880]{0:T(1024)(128)(4,1)} %bitcast.104), calls=%async_computation.4 | async-start | bytes 2097152
  87.8 4.6 %slice-start.2 = ((s8[5242880]{0:T(1024)(128)(4,1)}), s8[4194304]{0:T(1024)(128)(4,1)S(1)}, s32[]{:S(2)}) async-start(s8[5242880]{0:T(1024)(128)(4,1)} %bitcast.106), calls=%async_computation.5 | async-start | bytes 8388608
  89.4 3.0 %slice-start.3 = ((s8[5242880]{0:T(1024)(128)(4,1)}), s8[1048576]{0:T(1024)(128)(4,1)S(1)}, s32[]{:S(2)}) async-start(s8[5242880]{0:T(1024)(128)(4,1)} %bitcast.106), calls=%async_computation.6 | async-start | bytes 2097152
  90.9 3.0 %copy-start.9 = (bf16[256,5,64]{0,1,2:T(8,128)(2,1)S(1)}, bf16[256,5,64]{0,1,2:T(8,128)(2,1)}, u32[]{:S(2)}) copy-start(bf16[256,5,64]{0,1,2:T(8,128)(2,1)} %fusion.28) | copy-start | bytes 491524
  93.9 19.1 %copy-start.10 = (bf16[256,512]{1,0:T(8,128)(2,1)S(1)}, bf16[256,512]{1,0:T(8,128)(2,1)}, u32[]{:S(2)}) copy-start(bf16[256,512]{1,0:T(8,128)(2,1)} %param.10) | copy-start | bytes 786436
  93.9 20.2 %copy-start.11 = (bf16[2048]{0:T(1024)(128)(2,1)S(1)}, bf16[2048]{0:T(1024)(128)(2,1)}, u32[]{:S(2)}) copy-start(bf16[2048]{0:T(1024)(128)(2,1)} %param.15) | copy-start | bytes 12292
  94.3 8.9 %collective-permute-start = (bf16[256,320]{0,1:T(8,128)(2,1)S(1)}, bf16[256,320]{0,1:T(8,128)(2,1)S(1)}, u32[]{:S(2)}, u32[]{:S(2)}) collective-permute-start(bf16[256,320]{0,1:T(8,128)(2,1)S(1)} %bitcast.118), channel_id=1, source_target_pairs={{0,1},{1,2},{2,3},{3,0},{4,5},{5,6},{6,7},{7,4},{8,9},{9,10},{10,1... | collective-permute-start | bytes 491528 | tf_op jit(solution)/shard_map/ppermute | solution.py:51
  95.8 9.6 %collective-permute-start.4 = (bf16[256,320]{0,1:T(8,128)(2,1)S(1)}, bf16[256,320]{0,1:T(8,128)(2,1)S(1)}, u32[]{:S(2)}, u32[]{:S(2)}) collective-permute-start(bf16[256,320]{0,1:T(8,128)(2,1)S(1)} %bitcast.119), channel_id=1, source_target_pairs={{0,3},{1,0},{2,1},{3,2},{4,7},{5,4},{6,5},{7,6},{8,11},{9,8},{10,9... | collective-permute-start | bytes 491528 | tf_op jit(solution)/shard_map/ppermute | solution.py:51
  99.5 13.6 %collective-permute-start.2 = (bf16[256,320]{0,1:T(8,128)(2,1)S(1)}, bf16[256,320]{0,1:T(8,128)(2,1)S(1)}, u32[]{:S(2)}, u32[]{:S(2)}) collective-permute-start(bf16[256,320]{0,1:T(8,128)(2,1)S(1)} %bitcast.121), channel_id=1, source_target_pairs={{0,2},{1,3},{2,0},{3,1},{4,6},{5,7},{6,4},{7,5},{8,10},{9,11},{10,... | collective-permute-start | bytes 491528 | tf_op jit(solution)/shard_map/ppermute | solution.py:51
Sparse Core Ops, SparseCore 0:
  10.5 30.5 all-gather.8
  50.7 28.1 all-gather.4
  114.2 26.1 all-gather.6
where the time goes:
time: 151 us
  waiting for transfers between devices  65.7 us (44%)
  matrix products  37.2 us (25%)
  between operations  16.9 us (11%)
  local copies, waits for them, and re-layouts  11.6 us (8%)
  starting transfers between devices  10.9 us (7%)
  other arithmetic  8.57 us (6%)
    all_gather x2, waiting for transfers between devices, every_slot_of(): return lax.all_gather(part, 'req', axis=0, tiled=True)  29.2 us
    all_gather x1, waiting for transfers between devices, local(): full_new = lax.all_gather(new_residual, 'tp', axis=1, tiled=True)  26.2 us
    dot_general x8, matrix products, pick_part(): jnp.einsum('njd,hj->nhd', part_rows, select, preferred_element_type=jnp.f...  12.6 us
    ppermute x6, starting transfers between devices, shifted(): return lax.ppermute(block, 'tp', pairs)  10.6 us
    ppermute x6, waiting for transfers between devices, shifted(): return lax.ppermute(block, 'tp', pairs)  10.3 us
    dot_general x4, matrix products, local(): jnp.einsum('hrp,phd->rhd', prefix_weights.astype(jnp.bfloat16), picked[te...  8.43 us
    dot_general x4, matrix products, local(): jnp.einsum('rhd,phd->hrp', query_heads, picked[tenant_id][0], preferred_e...  6.74 us
    optimization_barrier x2, local copies, waits for them, and re-layouts, local(): own_values, every_key = lax.optimization_barrier((own_values, every_key))  4.73 us
  transfers between devices with their start and end apart: 9, of which 6 were waited for; matrix products, arithmetic and copies ran while one was open for 33% of the time, Pallas kernels for 0%

commit v1 on v0

--- a/solution.py
+++ b/solution.py
@@ -1,3 +1,4 @@
+import functools
 import jax
 import jax.numpy as jnp
 from jax import lax
@@ -8,6 +9,26 @@
 HD = 64
 TENANTS = 4
 GATHER_SLOTS_MAX = 16
+
+
+def chunk_show(field_in, dimension_no, named_axis):
+    view_out, outer, side_arr = (
+        lax.axis_size(named_axis),
+        lax.axis_index(named_axis),
+        field_in.shape[dimension_no],
+    )
+    newest, big = (field_in, 1)
+    while big < view_out:
+        by_place = []
+        for p in range(view_out):
+            by_place.append((p, (p - big) % view_out))
+        newest = jnp.concatenate([newest, lax.ppermute(newest, named_axis, by_place)], dimension_no)
+        big = 2 * big
+    last = jnp.roll(newest, outer * side_arr, dimension_no)
+    return last
+
+
+finish_boxes = functools.partial(chunk_show, dimension_no=0, named_axis="req")
 
 
 def from_root(block, axis, source):
@@ -27,7 +48,7 @@
 
 
 def every_slot_of(part, n_req):
-    return lax.all_gather(part, "req", axis=0, tiled=True)
+    return finish_boxes(part)
 
 
 def slots_of_tenants(part, every_slot, owners, n_req):

time: 151 us -> 209 us (1.38)
  waiting for transfers between devices: 65.7 us -> 101 us
  other arithmetic: 8.57 us -> 41.6 us
  matrix products: 37.2 us -> 24.1 us
  starting transfers between devices: 10.9 us -> 20 us
  local copies, waits for them, and re-layouts: 11.6 us -> 4.8 us
    ppermute x0 -> x6, waiting for transfers between devices: none -> 62.4 us  [chunk_show(): lax.ppermute(newest, named_axis, by_place)]
    concatenate x0 -> x6, other arithmetic: none -> 35.2 us  [the longest x2 31.8 us: chunk_show(): last = jnp.roll(newest, outer * side_arr, dimension_no)]
    all_gather x2 -> x0, waiting for transfers between devices: 29.2 us -> none  [every_slot_of(): return lax.all_gather(part, 'req', axis=0, tiled=True)]
    ppermute x0 -> x6, starting transfers between devices: none -> 10.3 us  [chunk_show(): lax.ppermute(newest, named_axis, by_place)]
    dot_general x8, matrix products: 12.6 us -> 5.14 us  [pick_part(): jnp.einsum('njd,hj->nhd', part_rows, select, preferred_element_type=jnp.f...]
    optimization_barrier x2 -> x1, local copies, waits for them, and re-layouts: 4.73 us -> 0.27 us  [local(): own_values, every_key = lax.optimization_barrier((own_values, every_key))]
    dot_general x4, matrix products: 8.43 us -> 5.75 us  [local(): jnp.einsum('hrp,phd->rhd', prefix_weights.astype(jnp.bfloat16), picked[te...]
  transfers between devices with their start and end apart: 9 -> 13, of which waited for: 6 -> 7; matrix products, arithmetic and copies ran while one was open for 33% -> 30% of each run, Pallas kernels for 0% -> 0%
where the time goes in v1:
time: 209 us
  waiting for transfers between devices  101 us (48%)
  other arithmetic  41.6 us (20%)
  matrix products  24.1 us (12%)
  starting transfers between devices  20 us (10%)
  between operations  17.1 us (8%)
  local copies, waits for them, and re-layouts  4.8 us (2%)
    ppermute x6, waiting for transfers between devices, chunk_show(): lax.ppermute(newest, named_axis, by_place)  62.4 us
    concatenate x2, other arithmetic, chunk_show(): last = jnp.roll(newest, outer * side_arr, dimension_no)  31.8 us
    all_gather x1, waiting for transfers between devices, local(): full_new = lax.all_gather(new_residual, 'tp', axis=1, tiled=True)  28.1 us
    ppermute x6, waiting for transfers between devices, shifted(): return lax.ppermute(block, 'tp', pairs)  10.8 us
    ppermute x6, starting transfers between devices, chunk_show(): lax.ppermute(newest, named_axis, by_place)  10.3 us
    ppermute x6, starting transfers between devices, shifted(): return lax.ppermute(block, 'tp', pairs)  9.68 us
    dot_general x4, matrix products, local(): jnp.einsum('hrp,phd->rhd', prefix_weights.astype(jnp.bfloat16), picked[te...  5.75 us
    dot_general x4, matrix products, local(): jnp.einsum('rhd,phd->hrp', query_heads, picked[tenant_id][0], preferred_e...  5.44 us
  transfers between devices with their start and end apart: 13, of which 7 were waited for; matrix products, arithmetic and copies ran while one was open for 30% of the time, Pallas kernels for 0%

profile of v1, /device:TPU:0, one launch (start us, length us, event | category | flops | bytes accessed | tf_op | source)
XLA Modules:
  0.0 208.9 jit_solution(6750652401001016375)
XLA Ops:
  7.2 0.0 copy-start
  7.2 0.0 all-gather.2.cloned.1.call-start
  7.3 1.3 copy.28
  8.6 0.0 copy-start.1
  8.7 0.3 copy.32
  8.9 3.4 %collective-permute-start = (bf16[1024,2,64]{0,1,2:T(2,128)(2,1)S(1)}, bf16[1024,2,64]{0,1,2:T(2,128)(2,1)S(1)}, u32[]{:S(2)}, u32[]{:S(2)}) collective-permute-start(bf16[1024,2,64]{0,1,2:T(2,128)(2,1)S(1)} %copy.32), channel_id=1, source_target_pairs={{0,28},{4,0},{8,4},{12,8},{16,12},{20,16},{24,20},{28,24},{1,29},{... | collective-permute-start | bytes 786440 | tf_op jit(solution)/shard_map/ppermute | solution.py:25
  12.3 2.1 constant_dynamic-slice_fusion.1
  14.4 3.6 %collective-permute-start.11 = (bf16[320,512]{1,0:T(8,128)(2,1)}, bf16[320,512]{1,0:T(8,128)(2,1)S(1)}, u32[]{:S(2)}, u32[]{:S(2)}) collective-permute-start(bf16[320,512]{1,0:T(8,128)(2,1)} %get-tuple-element.15), channel_id=1, source_target_pairs={{0,3},{1,0},{2,1},{3,2},{4,7},{5,4},{6,5},{7,6},{8,11},{9,8},{10,9... | collective-permute-start | bytes 983048 | tf_op jit(solution)/shard_map/ppermute | solution.py:72
  18.0 1.0 collective-permute-start.9
  19.0 0.2 reduce-window.4
  19.2 0.1 convert_reduce_fusion
  19.3 0.7 fusion.114
  22.5 0.1 copy.24
  22.7 0.5 pad_maximum_fusion.2
  23.2 0.7 collective-permute-start.1
  23.8 0.1 select_reduce_fusion.6
  24.0 10.8 %collective-permute-done.1 = bf16[2048,2,64]{0,1,2:T(2,128)(2,1)S(1)} collective-permute-done((bf16[2048,2,64]{0,1,2:T(2,128)(2,1)S(1)}, bf16[2048,2,64]{0,1,2:T(2,128)(2,1)S(1)}, u32[]{:S(2)}, u32[]{:S(2)}) %collective-permute-start.1) | collective-permute-done | bytes 524320 | tf_op jit(solution)/shard_map/ppermute | solution.py:25
  34.8 1.3 pad_maximum_fusion
  36.1 1.6 collective-permute-start.2
  37.7 0.3 fusion.36
  38.0 0.3 fusion.35
  38.3 0.4 select_reduce_fusion.4
  38.7 21.2 %collective-permute-done.2 = bf16[4096,2,64]{0,1,2:T(2,128)(2,1)S(1)} collective-permute-done((bf16[4096,2,64]{0,1,2:T(2,128)(2,1)S(1)}, bf16[4096,2,64]{0,1,2:T(2,128)(2,1)S(1)}, u32[]{:S(2)}, u32[]{:S(2)}) %collective-permute-start.2) | collective-permute-done | bytes 1048608 | tf_op jit(solution)/shard_map/ppermute | solution.py:25
  59.9 13.7 %fusion.17 = bf16[8192,2,64]{0,1,2:T(2,128)(2,1)S(1)} fusion(s32[]{:T(128)S(6)} %select_n.152, bf16[4096,2,64]{0,1,2:T(2,128)(2,1)S(1)} %collective-permute-done.2, bf16[2048,2,64]{0,1,2:T(2,128)(2,1)S(1)} %collective-permute-done.1, bf16[1024,2,64]{0,1,2:T(2,128)(2,1)S(1)} %collective-permute-done, bf16[1024,2,64]{0,1,2:T(2,128)(2,1)S(1)} %copy.32), kind=kLoop, calls=%fused_computation.44 | loop fusion | flops 16777216 | bytes 4194308 | tf_op jit(solution)/shard_map/jit(_roll_dynamic)/concatenate | solution.py:27
  73.6 0.5 fusion.22
  74.2 0.5 fusion.21
  74.7 0.5 fusion.20
  75.2 0.3 copy.42
  75.5 1.0 collective-permute-start.3
  76.5 1.3 select_reduce_fusion
  77.8 1.3 select_reduce_fusion.1
  79.2 1.4 select_reduce_fusion.2
  80.6 0.5 fusion.19
  81.1 0.5 pad_maximum_fusion.3
  81.6 2.7 %collective-permute-start.4 = (bf16[2048,2,64]{0,1,2:T(2,128)(2,1)S(1)}, bf16[2048,2,64]{0,1,2:T(2,128)(2,1)S(1)}, u32[]{:S(2)}, u32[]{:S(2)}) collective-permute-start(bf16[2048,2,64]{0,1,2:T(2,128)(2,1)S(1)} %pad_maximum_fusion.3), channel_id=1, source_target_pairs={{0,24},{4,28},{8,0},{12,4},{16,8},{20,12},{24,16},{28,20},{1,25},{... | collective-permute-start | bytes 1572872 | tf_op jit(solution)/shard_map/ppermute | solution.py:25
  84.3 1.4 select_reduce_fusion.3
  85.7 0.2 fusion.38
  85.9 10.3 %collective-permute-done.4 = bf16[2048,2,64]{0,1,2:T(2,128)(2,1)S(1)} collective-permute-done((bf16[2048,2,64]{0,1,2:T(2,128)(2,1)S(1)}, bf16[2048,2,64]{0,1,2:T(2,128)(2,1)S(1)}, u32[]{:S(2)}, u32[]{:S(2)}) %collective-permute-start.4) | collective-permute-done | bytes 524320 | tf_op jit(solution)/shard_map/ppermute | solution.py:25
  96.2 1.2 pad_maximum_fusion.1
  97.4 1.0 collective-permute-start.5
  98.4 4.1 %bitcast_reduce_fusion.3 = (f32[5,256]{1,0:T(8,128)S(1)}, f32[5,256]{1,0:T(8,128)S(1)}, f32[5,256]{1,0:T(8,128)S(1)}, f32[5,256]{1,0:T(8,128)S(1)}) fusion(f32[5,1024,256]{2,1,0:T(8,128)S(1)} %get-tuple-element.37, f32[5,256]{1,0:T(8,128)S(1)} %maximum_maximum_fusion.1, pred[256]{0:T(512)(128)(4,1)S(1)} %get-tuple-element.20, ...), kind=kLoop, calls=%fused_computation.6 | loop fusion | flops 20966400 | bytes 20998144 | tf_op jit(solution)/shard_map/reduce_sum | solution.py:170
  102.5 20.1 %collective-permute-done.5 = bf16[4096,2,64]{0,1,2:T(2,128)(2,1)S(1)} collective-permute-done((bf16[4096,2,64]{0,1,2:T(2,128)(2,1)S(1)}, bf16[4096,2,64]{0,1,2:T(2,128)(2,1)S(1)}, u32[]{:S(2)}, u32[]{:S(2)}) %collective-permute-start.5) | collective-permute-done | bytes 1048608 | tf_op jit(solution)/shard_map/ppermute | solution.py:25
  122.7 18.1 %maximum_maximum_fusion = bf16[16384,2,64]{0,1,2:T(2,128)(2,1)S(1)} fusion(bf16[4096,2,64]{0,1,2:T(2,128)(2,1)S(1)} %collective-permute-done.5, bf16[2048,2,64]{0,1,2:T(2,128)(2,1)S(1)} %collective-permute-done.4, bf16[1024,2,64]{0,1,2:T(2,128)(2,1)S(1)} %collective-permute-done.3, bf16[1024,2,64]{0,1,2:T(2,128)(2,1)S(1)} %copy.42), kind=kLoop, calls=%fused_computation.24 | loop fusion | flops 33554432 | bytes 6291456 | tf_op jit(solution)/shard_map/jit(_roll_dynamic)/concatenate | solution.py:27
  140.8 0.8 fusion.26
  141.5 1.4 fusion.3
  143.0 0.8 fusion.25
  143.8 1.4 fusion.2
  145.2 0.8 fusion.24
  146.0 1.4 fusion.1
  147.4 0.8 fusion.23
  148.2 1.4 fusion
  149.6 0.3 fusion.37
  150.0 3.9 %collective-permute-start.10 = (bf16[256,320]{0,1:T(8,128)(2,1)S(1)}, bf16[256,320]{0,1:T(8,128)(2,1)S(1)}, u32[]{:S(2)}, u32[]{:S(2)}) collective-permute-start(bf16[256,320]{0,1:T(8,128)(2,1)S(1)} %bitcast.112), channel_id=1, source_target_pairs={{0,3},{1,0},{2,1},{3,2},{4,7},{5,4},{6,5},{7,6},{8,11},{9,8},{10,9... | collective-permute-start | bytes 491528 | tf_op jit(solution)/shard_map/ppermute | solution.py:72
  153.8 1.3 fusion.59
  155.1 1.2 collective-permute-start.8
  156.3 6.5 %collective-permute-done.6 = bf16[256,320]{0,1:T(8,128)(2,1)S(1)} collective-permute-done((bf16[256,320]{0,1:T(8,128)(2,1)S(1)}, bf16[256,320]{0,1:T(8,128)(2,1)S(1)}, u32[]{:S(2)}, u32[]{:S(2)}) %collective-permute-start.6) | collective-permute-done | bytes 163872 | tf_op jit(solution)/shard_map/ppermute | solution.py:72
  162.9 1.3 convolution_add_fusion.1
  164.2 0.3 fusion.115
  164.5 4.2 %collective-permute-done.8 = bf16[256,320]{0,1:T(8,128)(2,1)S(1)} collective-permute-done((bf16[256,320]{0,1:T(8,128)(2,1)S(1)}, bf16[256,320]{0,1:T(8,128)(2,1)S(1)}, u32[]{:S(2)}, u32[]{:S(2)}) %collective-permute-start.8) | collective-permute-done | bytes 163872 | tf_op jit(solution)/shard_map/ppermute | solution.py:72
  168.8 1.1 fusion.29
  169.8 0.0 all-gather.2.cloned.1.call-update
  169.9 28.1 %all-gather.2.cloned.1.call-done = bf16[256,2048]{1,0:T(8,128)(2,1)} async-done(((bf16[256,512]{1,0:T(8,128)(2,1)}), bf16[256,2048]{1,0:T(8,128)(2,1)}) %all-gather.2.cloned.1.call-update) | async-done | bytes 1048592 | tf_op jit(solution)/shard_map/all_gather | solution.py:189
  198.0 1.5 fusion.14
  199.5 2.5 %convolution_convert_fusion.10 = bf16[256,320]{0,1:T(8,128)(2,1)} fusion(bf16[2048,320]{0,1:T(8,128)(2,1)S(1)} %copy-done, bf16[256,2048]{1,0:T(8,128)(2,1)} %all-gather.2.cloned.1.call-done, f32[2048]{0:T(1024)S(1)} %convert_element_type.130, f32[256]{0:T(256)S(1)} %add_rsqrt_fusion), kind=kOutput, calls=%fused_computation.81 | convolution fusion | flops 337723392 | bytes 2532352 | tf_op jit(solution)/shard_map/dot_general | solution.py:195
  (32 shorter events, 0.2 us)
Async XLA Ops:
  7.2 192.3 %copy-start = (bf16[2048,320]{0,1:T(8,128)(2,1)S(1)}, bf16[2048,320]{0,1:T(8,128)(2,1)}, u32[]{:S(2)}) copy-start(bf16[2048,320]{0,1:T(8,128)(2,1)} %param.18) | copy-start | bytes 3932164
  7.2 11.8 %copy-start.7 = (s32[1,4]{1,0:T(1,128)S(1)}, s32[1,4]{1,0:T(1,128)}, u32[]{:S(2)}) copy-start(s32[1,4]{1,0:T(1,128)} %param.19) | copy-start | bytes 52
  7.2 12.1 %copy-start.4 = (s32[4]{0:T(128)S(1)}, s32[4]{0:T(128)}, u32[]{:S(2)}) copy-start(s32[4]{0:T(128)} %param.21) | copy-start | bytes 52
  7.2 15.3 %copy-start.3 = (bf16[256,1,256]{2,0,1:T(8,128)(2,1)S(1)}, bf16[256,1,256]{2,0,1:T(8,128)(2,1)}, u32[]{:S(2)}) copy-start(bf16[256,1,256]{2,0,1:T(8,128)(2,1)} %param.14) | copy-start | bytes 393220
  7.2 16.6 %copy-start.6 = (s32[1,4]{1,0:T(1,128)S(1)}, s32[1,4]{1,0:T(1,128)}, u32[]{:S(2)}) copy-start(s32[1,4]{1,0:T(1,128)} %param.20) | copy-start | bytes 52
  7.2 190.8 %all-gather.2.cloned.1.call-start = ((), (), s32[]{:S(2)}) async-start(), calls=%async_computation | async-start | bytes 1310720 | tf_op jit(solution)/shard_map/all_gather | solution.py:189
  8.6 29.7 %copy-start.1 = (bf16[256,320]{0,1:T(8,128)(2,1)S(1)}, bf16[256,320]{0,1:T(8,128)(2,1)}, u32[]{:S(2)}) copy-start(bf16[256,320]{0,1:T(8,128)(2,1)} %param.13) | copy-start | bytes 491524
  8.9 13.7 %collective-permute-start = (bf16[1024,2,64]{0,1,2:T(2,128)(2,1)S(1)}, bf16[1024,2,64]{0,1,2:T(2,128)(2,1)S(1)}, u32[]{:S(2)}, u32[]{:S(2)}) collective-permute-start(bf16[1024,2,64]{0,1,2:T(2,128)(2,1)S(1)} %copy.32), channel_id=1, source_target_pairs={{0,28},{4,0},{8,4},{12,8},{16,12},{20,16},{24,20},{28,24},{1,29},{... | collective-permute-start | bytes 786440 | tf_op jit(solution)/shard_map/ppermute | solution.py:25
  14.4 149.8 %collective-permute-start.11 = (bf16[320,512]{1,0:T(8,128)(2,1)}, bf16[320,512]{1,0:T(8,128)(2,1)S(1)}, u32[]{:S(2)}, u32[]{:S(2)}) collective-permute-start(bf16[320,512]{1,0:T(8,128)(2,1)} %get-tuple-element.15), channel_id=1, source_target_pairs={{0,3},{1,0},{2,1},{3,2},{4,7},{5,4},{6,5},{7,6},{8,11},{9,8},{10,9... | collective-permute-start | bytes 983048 | tf_op jit(solution)/shard_map/ppermute | solution.py:72
  18.0 137.1 %collective-permute-start.7 = (bf16[320,512]{1,0:T(8,128)(2,1)}, bf16[320,512]{1,0:T(8,128)(2,1)}, u32[]{:S(2)}, u32[]{:S(2)}) collective-permute-start(bf16[320,512]{1,0:T(8,128)(2,1)} %get-tuple-element.14), channel_id=1, source_target_pairs={{0,1},{1,2},{2,3},{3,0},{4,5},{5,6},{6,7},{7,4},{8,9},{9,10},{10,1... | collective-permute-start | bytes 983048 | tf_op jit(solution)/shard_map/ppermute | solution.py:72
  18.0 146.5 %collective-permute-start.9 = (bf16[320,512]{1,0:T(8,128)(2,1)S(1)}, bf16[320,512]{1,0:T(8,128)(2,1)S(1)}, u32[]{:S(2)}, u32[]{:S(2)}) collective-permute-start(bf16[320,512]{1,0:T(8,128)(2,1)S(1)} %get-tuple-element.13), channel_id=1, source_target_pairs={{0,2},{1,3},{2,0},{3,1},{4,6},{5,7},{6,4},{7,5},{8,10},{9,11},{10,... | collective-permute-start | bytes 983048 | tf_op jit(solution)/shard_map/ppermute | solution.py:72
  23.2 11.7 %collective-permute-start.1 = (bf16[2048,2,64]{0,1,2:T(2,128)(2,1)S(1)}, bf16[2048,2,64]{0,1,2:T(2,128)(2,1)S(1)}, u32[]{:S(2)}, u32[]{:S(2)}) collective-permute-start(bf16[2048,2,64]{0,1,2:T(2,128)(2,1)S(1)} %pad_maximum_fusion.2), channel_id=1, source_target_pairs={{0,24},{4,28},{8,0},{12,4},{16,8},{20,12},{24,16},{28,20},{1,25},{... | collective-permute-start | bytes 1572872 | tf_op jit(solution)/shard_map/ppermute | solution.py:25
  36.1 23.8 %collective-permute-start.2 = (bf16[4096,2,64]{0,1,2:T(2,128)(2,1)S(1)}, bf16[4096,2,64]{0,1,2:T(2,128)(2,1)S(1)}, u32[]{:S(2)}, u32[]{:S(2)}) collective-permute-start(bf16[4096,2,64]{0,1,2:T(2,128)(2,1)S(1)} %pad_maximum_fusion), channel_id=1, source_target_pairs={{0,16},{4,20},{8,24},{12,28},{16,0},{20,4},{24,8},{28,12},{1,17},{... | collective-permute-start | bytes 3145736 | tf_op jit(solution)/shard_map/ppermute | solution.py:25
  75.5 5.6 %collective-permute-start.3 = (bf16[1024,2,64]{0,1,2:T(2,128)(2,1)S(1)}, bf16[1024,2,64]{0,1,2:T(2,128)(2,1)S(1)}, u32[]{:S(2)}, u32[]{:S(2)}) collective-permute-start(bf16[1024,2,64]{0,1,2:T(2,128)(2,1)S(1)} %copy.42), channel_id=1, source_target_pairs={{0,28},{4,0},{8,4},{12,8},{16,12},{20,16},{24,20},{28,24},{1,29},{... | collective-permute-start | bytes 786440 | tf_op jit(solution)/shard_map/ppermute | solution.py:25
  81.6 14.6 %collective-permute-start.4 = (bf16[2048,2,64]{0,1,2:T(2,128)(2,1)S(1)}, bf16[2048,2,64]{0,1,2:T(2,128)(2,1)S(1)}, u32[]{:S(2)}, u32[]{:S(2)}) collective-permute-start(bf16[2048,2,64]{0,1,2:T(2,128)(2,1)S(1)} %pad_maximum_fusion.3), channel_id=1, source_target_pairs={{0,24},{4,28},{8,0},{12,4},{16,8},{20,12},{24,16},{28,20},{1,25},{... | collective-permute-start | bytes 1572872 | tf_op jit(solution)/shard_map/ppermute | solution.py:25
  97.4 25.2 %collective-permute-start.5 = (bf16[4096,2,64]{0,1,2:T(2,128)(2,1)S(1)}, bf16[4096,2,64]{0,1,2:T(2,128)(2,1)S(1)}, u32[]{:S(2)}, u32[]{:S(2)}) collective-permute-start(bf16[4096,2,64]{0,1,2:T(2,128)(2,1)S(1)} %pad_maximum_fusion.1), channel_id=1, source_target_pairs={{0,16},{4,20},{8,24},{12,28},{16,0},{20,4},{24,8},{28,12},{1,17},{... | collective-permute-start | bytes 3145736 | tf_op jit(solution)/shard_map/ppermute | solution.py:25
  149.6 19.2 %copy-start.2 = (bf16[256,512]{1,0:T(8,128)(2,1)S(1)}, bf16[256,512]{1,0:T(8,128)(2,1)}, u32[]{:S(2)}) copy-start(bf16[256,512]{1,0:T(8,128)(2,1)} %param.12) | copy-start | bytes 786436
  149.6 20.2 %copy-start.5 = (bf16[2048]{0:T(1024)(128)(2,1)S(1)}, bf16[2048]{0:T(1024)(128)(2,1)}, u32[]{:S(2)}) copy-start(bf16[2048]{0:T(1024)(128)(2,1)} %param.17) | copy-start | bytes 12292
  150.0 14.2 %collective-permute-start.10 = (bf16[256,320]{0,1:T(8,128)(2,1)S(1)}, bf16[256,320]{0,1:T(8,128)(2,1)S(1)}, u32[]{:S(2)}, u32[]{:S(2)}) collective-permute-start(bf16[256,320]{0,1:T(8,128)(2,1)S(1)} %bitcast.112), channel_id=1, source_target_pairs={{0,3},{1,0},{2,1},{3,2},{4,7},{5,4},{6,5},{7,6},{8,11},{9,8},{10,9... | collective-permute-start | bytes 491528 | tf_op jit(solution)/shard_map/ppermute | solution.py:72
  153.8 9.0 %collective-permute-start.6 = (bf16[256,320]{0,1:T(8,128)(2,1)S(1)}, bf16[256,320]{0,1:T(8,128)(2,1)S(1)}, u32[]{:S(2)}, u32[]{:S(2)}) collective-permute-start(bf16[256,320]{0,1:T(8,128)(2,1)S(1)} %bitcast.113), channel_id=1, source_target_pairs={{0,1},{1,2},{2,3},{3,0},{4,5},{5,6},{6,7},{7,4},{8,9},{9,10},{10,1... | collective-permute-start | bytes 491528 | tf_op jit(solution)/shard_map/ppermute | solution.py:72
  155.1 13.6 %collective-permute-start.8 = (bf16[256,320]{0,1:T(8,128)(2,1)S(1)}, bf16[256,320]{0,1:T(8,128)(2,1)S(1)}, u32[]{:S(2)}, u32[]{:S(2)}) collective-permute-start(bf16[256,320]{0,1:T(8,128)(2,1)S(1)} %bitcast.115), channel_id=1, source_target_pairs={{0,2},{1,3},{2,0},{3,1},{4,6},{5,7},{6,4},{7,5},{8,10},{9,11},{10,... | collective-permute-start | bytes 491528 | tf_op jit(solution)/shard_map/ppermute | solution.py:72
Sparse Core Ops, SparseCore 0:
  170.0 27.9 all-gather.1
